TPU v7x, 128 devices: a whole 4x4x4 slice. The times are simulated.
128 devices in a mesh: req: 16 (over y, x), kvh: 8 (over z, core).
Axes of the slice: x: 4, y: 4, z: 4, core: 2. Of those that a mesh axis runs over, the one named last changes fastest.
Arguments:
- states: bfloat16 [128, 2560], P('req', 'kvh'), may hold values from -6 to 6
- attn_gain: bfloat16 [2560], replicated, may hold values from 0.099609375 to 1.8984375
- w_query: bfloat16 [2560, 4096], P(None, 'kvh'), may hold values from -0.125 to 0.125
- w_key: bfloat16 [2560, 1024], P(None, 'kvh'), may hold values from -0.125 to 0.125
- w_value: bfloat16 [2560, 1024], P(None, 'kvh'), may hold values from -0.125 to 0.125
- query_gain: bfloat16 [128], replicated, may hold values from 0.5 to 2
- key_gain: bfloat16 [128], replicated, may hold values from 0.5 to 2
- w_output: bfloat16 [4096, 2560], P('kvh'), may hold values from -0.25 to 0.25
- ffn_gain: bfloat16 [2560], P('kvh'), may hold values from 0.099609375 to 1.8984375
- w_gate: bfloat16 [2560, 9728], P('kvh', 'req'), may hold values from -0.125 to 0.125
- w_up: bfloat16 [2560, 9728], P('kvh', 'req'), may hold values from -0.125 to 0.125
- w_down: bfloat16 [9728, 2560], P('req', 'kvh'), may hold values from -0.0625 to 0.0625
- kv_pool: bfloat16 [1024, 8, 128, 256], P('req', 'kvh'), may hold values from -6 to 6
- lengths: int32 [128], replicated, may hold values from 1 to 1023, as said below
- page_table: int32 [128, 8], P('req'), may hold values from 0 to 63, as said below
- new_order: int32 [128], replicated, may hold values from 0 to 127, as said below
Outputs:
- output: bfloat16 [128, 2560], P('req', 'kvh')
- new_pool: bfloat16 [1024, 8, 128, 256], P('req', 'kvh')
Inputs may be any that keep to these rules, and one draw needn't show every extreme that they name: `lengths`: each request has at least one cached position and room for the new one; some request has exactly 1023. `page_table`: the 8 rows of one device name each of its 64 pool rows exactly once. `new_order`: A permutation of the requests; slot s lies on the device s // 8. The 8 requests of one device go to 8 different devices, and each device receives its 8 requests from 8 different devices.
All inputs are finite; a program needn't handle non-finite values.
Results may differ from a plain program's by a relative error of at most 0.0087.
Values may be sent and summed in bfloat16 or wider, within the bound.
No kernel may reach another device: no remote copies, remote signals or barrier semaphores. Data moves between devices by JAX's collectives and lax.ppermute only.
A program may use at most 128 MiB of HBM per device.

v0:
```python
import math
import jax
import jax.numpy as jnp
from jax import lax
from jax.sharding import PartitionSpec as P

D = 2560
EPSILON = 1e-06


def rms_norm(values, norm_gain):
    mean_sq = jnp.mean(values * values, axis=-1, keepdims=True)
    return values * lax.rsqrt(mean_sq + EPSILON) * norm_gain


def rotary(values, positions):
    half_dim = values.shape[-1] // 2
    frequency = jnp.exp(
        jnp.arange(half_dim, dtype=jnp.float32) * (-2.0 * math.log(1000000.0) / values.shape[-1])
    )
    angles = positions.astype(jnp.float32)[:, None, None] * frequency
    cosine = jnp.cos(angles)
    sine_part = jnp.sin(angles)
    first_half = values[..., :half_dim]
    second_half = values[..., half_dim:]
    return jnp.concatenate(
        [
            first_half * cosine - second_half * sine_part,
            second_half * cosine + first_half * sine_part,
        ],
        axis=-1,
    )


def mask_blocks(blocks, lengths_now, fresh):
    row_count, pages_per, kv_local, page_len, channels = blocks.shape
    positions = (
        jnp.arange(pages_per, dtype=jnp.int32)[:, None] * page_len
        + jnp.arange(page_len, dtype=jnp.int32)[None, :]
    )
    positions = positions[None, :, None, :, None]
    lengths_col = lengths_now[:, None, None, None, None]
    kept = positions < lengths_col
    placed = positions == lengths_col
    return jnp.where(
        kept, blocks, jnp.where(placed, fresh[:, None, :, None, :], jnp.zeros((), jnp.bfloat16))
    )


def attend(query, sequence, lengths_now):
    row_count, kv_local, span_len, channels = sequence.shape
    head_dim = channels // 2
    q_local = query.shape[1]
    group_size = q_local // kv_local
    grouped = query.reshape(row_count, kv_local, group_size, head_dim)
    scores = jnp.einsum(
        "rkgd,rktd->rkgt", grouped, sequence[..., :head_dim], preferred_element_type=jnp.float32
    ) * (1.0 / math.sqrt(head_dim))
    positions = jnp.arange(span_len, dtype=jnp.int32)
    valid = positions[None, None, None, :] <= lengths_now[:, None, None, None]
    scores = jnp.where(valid, scores, -jnp.inf)
    weights = jax.nn.softmax(scores, axis=-1).astype(jnp.bfloat16)
    mixed = jnp.einsum(
        "rkgt,rktd->rkgd", weights, sequence[..., head_dim:], preferred_element_type=jnp.float32
    )
    return mixed.reshape(row_count, q_local * head_dim).astype(jnp.bfloat16)


def per_device(
    states,
    attn_gain,
    w_query,
    w_key,
    w_value,
    query_gain,
    key_gain,
    w_output,
    ffn_gain,
    w_gate,
    w_up,
    w_down,
    kv_pool,
    lengths,
    page_table,
    new_order,
):
    devices_req = lax.axis_size("req")
    my_index = lax.axis_index("req")
    kvh_index = lax.axis_index("kvh")
    row_count = states.shape[0]
    width_local = states.shape[1]
    head_dim = query_gain.shape[0]
    kv_local = w_key.shape[1] // head_dim
    q_local = w_query.shape[1] // head_dim
    pages_per = page_table.shape[1]
    page_len = kv_pool.shape[2]
    channels = 2 * head_dim
    total_rows = new_order.shape[0]
    everyone = jnp.arange(total_rows, dtype=jnp.int32)
    new_position = jnp.zeros((total_rows,), jnp.int32).at[new_order].set(everyone)
    home = my_index * row_count + jnp.arange(row_count, dtype=jnp.int32)
    destination = new_position[home] // row_count
    peer_ids = jnp.arange(devices_req, dtype=jnp.int32)
    matches = destination[None, :] == peer_ids[:, None]
    picked = jnp.argmax(matches.astype(jnp.int32), axis=1)
    parcels = kv_pool[page_table[picked]]
    received = lax.all_to_all(parcels, "req", split_axis=0, concat_axis=0, tiled=True)
    arriving = lax.dynamic_slice_in_dim(new_order, my_index * row_count, row_count)
    source_owner = arriving // row_count
    full_states = lax.all_gather(states, "kvh", axis=1, tiled=True)
    normed = rms_norm(full_states.astype(jnp.float32), attn_gain.astype(jnp.float32)).astype(
        jnp.bfloat16
    )
    query = jnp.dot(normed, w_query, preferred_element_type=jnp.float32).reshape(
        row_count, q_local, head_dim
    )
    key_new = jnp.dot(normed, w_key, preferred_element_type=jnp.float32).reshape(
        row_count, kv_local, head_dim
    )
    value_new = jnp.dot(normed, w_value, preferred_element_type=jnp.float32).reshape(
        row_count, kv_local, head_dim
    )
    positions_home = lengths[home]
    query = rotary(rms_norm(query, query_gain.astype(jnp.float32)), positions_home).astype(
        jnp.bfloat16
    )
    key_new = rotary(rms_norm(key_new, key_gain.astype(jnp.float32)), positions_home).astype(
        jnp.bfloat16
    )
    fresh = jnp.concatenate([key_new, value_new.astype(jnp.bfloat16)], axis=-1)
    home_blocks = mask_blocks(kv_pool[page_table], positions_home, fresh)
    sequence = home_blocks.transpose(0, 2, 1, 3, 4).reshape(
        row_count, kv_local, pages_per * page_len, channels
    )
    mixed = attend(query, sequence, positions_home)
    partial_out = jnp.dot(mixed, w_output, preferred_element_type=jnp.float32)
    attn_out = lax.psum(partial_out, "kvh")
    residual_full = (full_states.astype(jnp.float32) + attn_out).astype(jnp.bfloat16)
    residual_wide_full = residual_full.astype(jnp.float32)
    total_sq = jnp.sum(residual_wide_full * residual_wide_full, axis=-1, keepdims=True)
    residual_wide = lax.dynamic_slice_in_dim(
        residual_wide_full, kvh_index * width_local, width_local, axis=1
    )
    normed_two = (
        residual_wide * lax.rsqrt(total_sq / D + EPSILON) * ffn_gain.astype(jnp.float32)
    ).astype(jnp.bfloat16)
    fresh_flat = fresh.reshape(row_count, kv_local * channels)
    gathered = lax.all_gather(
        jnp.concatenate([normed_two, fresh_flat], axis=1), "req", axis=0, tiled=True
    )
    normed_all = gathered[:, :width_local]
    fresh_all = gathered[:, width_local:].reshape(total_rows, kv_local, channels)
    ffn_width = w_gate.shape[1]
    joined = jnp.concatenate([w_gate, w_up], axis=1)
    partial_both = jnp.dot(normed_all, joined, preferred_element_type=jnp.float32)
    summed = lax.psum(partial_both, "kvh")
    hidden = (jax.nn.silu(summed[:, :ffn_width]) * summed[:, ffn_width:]).astype(jnp.bfloat16)
    lowered = lax.psum_scatter(
        jnp.dot(hidden, w_down, preferred_element_type=jnp.float32),
        "req",
        scatter_dimension=0,
        tiled=True,
    )
    result = (residual_wide + lowered).astype(jnp.bfloat16)
    arrived = received[source_owner]
    new_blocks = mask_blocks(arrived, lengths[arriving], fresh_all[arriving])
    new_pool = new_blocks.reshape(row_count * pages_per, kv_local, page_len, channels)
    return (result, new_pool)


def solution(mesh):
    in_specs = (
        P("req", "kvh"),
        P(),
        P(None, "kvh"),
        P(None, "kvh"),
        P(None, "kvh"),
        P(),
        P(),
        P("kvh", None),
        P("kvh"),
        P("kvh", "req"),
        P("kvh", "req"),
        P("req", "kvh"),
        P("req", "kvh", None, None),
        P(),
        P("req", None),
        P(),
    )
    out_specs = (P("req", "kvh"), P("req", "kvh", None, None))
    return jax.shard_map(
        per_device, mesh=mesh, in_specs=in_specs, out_specs=out_specs, check_vma=False
    )
```

profile of v0, /device:TPU:0, one launch (start us, length us, event | category | flops | bytes accessed | tf_op | source)
XLA Modules:
  0.0 340.9 jit_solution(16654045882225741350)
XLA Ops:
  7.2 0.8 compare_select_fusion.4
  8.0 1.0 scatter_custom_fusion
  9.0 0.6 gather_fusion.3
  10.3 1.2 gather_fusion.4
  11.8 8.7 %gather_fusion.5 = bf16[128,128,256]{2,1,0:T(8,128)(2,1)} fusion(bf16[64,128,256]{2,1,0:T(8,128)(2,1)} %bitcast.79, s32[1024]{0:T(1024)S(1)} %pad_clamp_fusion.1), kind=kCustom, calls=%fused_computation.5 | custom fusion | bytes 16777728 | tf_op jit(solution)/shard_map/gather | solution.py:106
  20.5 7.3 %all-to-all-start = ((bf16[16,8,1,128,256]{4,3,1,2,0:T(8,128)(2,1)}), bf16[16,8,1,128,256]{4,3,1,2,0:T(8,128)(2,1)}, u32[]{:S(2)}, u32[]{:S(2)}) async-start(bf16[16,8,1,128,256]{4,3,1,2,0:T(8,128)(2,1)} %bitcast.81), calls=%async_computation | async-start | bytes 16777216 | tf_op jit(solution)/shard_map/all_to_all | solution.py:107
  28.7 14.0 %all-gather = bf16[8,320,8]{1,2,0:T(8,128)(2,1)S(1)} all-gather(bf16[1,320,8]{1,2,0:T(8,128)(2,1)S(1)} %bitcast.84), channel_id=1, replica_groups=mesh['req'=16,'kvh'=8] {'kvh'}, dimensions={0}, use_global_device_ids=true | all-gather | bytes 46080 | tf_op jit(solution)/shard_map/all_gather | solution.py:110
  43.1 2.3 multiply_reduce_fusion.1
  45.4 5.1 %gather_fusion.1 = bf16[64,128,256]{2,1,0:T(8,128)(2,1)} fusion(bf16[64,128,256]{2,1,0:T(8,128)(2,1)} %bitcast.80, s32[1024]{0:T(1024)S(1)} %pad_clamp_fusion.4), kind=kCustom, calls=%fused_computation.1 | custom fusion | bytes 8388864 | tf_op jit(solution)/shard_map/gather | solution.py:131
  50.8 1.4 multiply_reduce_fusion.2
  52.9 7.6 %select_select_fusion.1 = bf16[8,1,1024,256]{3,2,0,1:T(8,128)(2,1)} fusion(bf16[8,1,1024,256]{3,2,0,1:T(8,128)(2,1)} %bitcast.83, pred[8,1024]{1,0:T(8,128)(4,1)S(1)} %get-tuple-element.13, pred[8,1024]{1,0:T(8,128)(4,1)S(1)} %get-tuple-element.12, bf16[8,256]{1,0:T(8,128)(2,1)S(1)} %maximum_bitcast_fusion), kind=kLoop, calls=%fused_computation.11 | loop fusion | flops 4194304 | bytes 8409088 | tf_op jit(solution)/shard_map/jit(_where)/select_n | solution.py:45
  60.6 2.5 fusion.48
  63.1 2.0 fusion.8
  65.1 1.1 fusion.26
  68.5 56.2 %all-reduce.5.cloned.1.call-done = f32[8,2560]{1,0:T(8,128)} async-done(((f32[8,2560]{1,0:T(8,128)}), f32[8,2560]{1,0:T(8,128)}) %all-reduce.5.cloned.1.call-update) | async-done | bytes 81936 | tf_op jit(solution)/shard_map/psum | solution.py:137
  124.7 1.0 multiply_reduce_fusion
  125.9 41.0 %all_gather.7 = bf16[128,576]{1,0:T(8,128)(2,1)S(1)} all-gather(bf16[8,576]{1,0:T(8,128)(2,1)S(1)} %pad_maximum_fusion), channel_id=1, replica_groups=mesh['req'=16,'kvh'=8] {'req'}, dimensions={0}, use_global_device_ids=true | all-gather | bytes 156672 | tf_op jit(solution)/shard_map/all_gather | solution.py:148
  166.9 2.7 fusion.10
  170.4 62.3 %all-reduce.7.cloned.1.call-done = f32[128,1216]{0,1:T(8,128)} async-done(((f32[128,1216]{0,1:T(8,128)}), f32[128,1216]{0,1:T(8,128)}) %all-reduce.7.cloned.1.call-update) | async-done | bytes 622608 | tf_op jit(solution)/shard_map/psum | solution.py:156
  232.8 2.2 fusion.15
  235.0 84.2 %all-reduce.9.cloned.1.call-done = f32[128,320]{1,0:T(8,128)} async-done(((f32[128,320]{1,0:T(8,128)}), f32[128,320]{1,0:T(8,128)}) %all-reduce.9.cloned.1.call-update) | async-done | bytes 163856
  319.2 1.4 fusion.25
  320.5 6.2 %gather_fusion.6 = bf16[8,8,128,256]{3,2,1,0:T(8,128)(2,1)} fusion(bf16[16,8,128,256]{3,2,1,0:T(8,128)(2,1)} %bitcast.16, s32[1024]{0:T(1024)S(1)} %pad_clamp_fusion), kind=kCustom, calls=%fused_computation.6 | custom fusion | bytes 8388640 | tf_op jit(solution)/shard_map/gather | solution.py:165
  326.7 7.6 %select_select_fusion = bf16[64,1,128,256]{3,2,1,0:T(8,128)(2,1)} fusion(bf16[64,1,128,256]{3,2,1,0:T(8,128)(2,1)} %bitcast.82, pred[64,128]{1,0:T(8,128)(4,1)S(1)} %get-tuple-element.11, pred[64,128]{1,0:T(8,128)(4,1)S(1)} %get-tuple-element.10, bf16[64,256]{1,0:T(8,128)(2,1)S(1)} %broadcast_bitcast_fusion), kind=kLoop, calls=%fused_computation.10 | loop fusion | flops 4194304 | bytes 8437760 | tf_op jit(solution)/shard_map/jit(_where)/select_n | solution.py:45
  (85 shorter events, 5.6 us)
Async XLA Ops:
  7.2 57.9 %copy-start = (bf16[512,2560]{1,0:T(8,128)(2,1)S(1)}, bf16[512,2560]{1,0:T(8,128)(2,1)}, u32[]{:S(2)}) copy-start(bf16[512,2560]{1,0:T(8,128)(2,1)} %param.23) | copy-start | bytes 7864324
  20.5 7.4 %copy-start.9 = (bf16[128]{0:T(256)(128)(2,1)S(1)}, bf16[128]{0:T(256)(128)(2,1)}, u32[]{:S(2)}) copy-start(bf16[128]{0:T(256)(128)(2,1)} %param.21) | copy-start | bytes 772
  20.5 7.5 %copy-start.10 = (bf16[128]{0:T(256)(128)(2,1)S(1)}, bf16[128]{0:T(256)(128)(2,1)}, u32[]{:S(2)}) copy-start(bf16[128]{0:T(256)(128)(2,1)} %param.22) | copy-start | bytes 772
  20.5 7.5 %copy-start.1 = (s32[128]{0:T(128)S(1)}, s32[128]{0:T(128)}, u32[]{:S(2)}) copy-start(s32[128]{0:T(128)} %param.29) | copy-start | bytes 1540
  20.5 8.1 %copy-start.2 = (s32[8,8]{1,0:T(8,128)S(1)}, s32[8,8]{1,0:T(8,128)}, u32[]{:S(2)}) copy-start(s32[8,8]{1,0:T(8,128)} %param.30) | copy-start | bytes 772
  20.5 8.2 %copy-start.5 = (bf16[2560]{0:T(1024)(128)(2,1)S(1)}, bf16[2560]{0:T(1024)(128)(2,1)}, u32[]{:S(2)}) copy-start(bf16[2560]{0:T(1024)(128)(2,1)} %param.17) | copy-start | bytes 15364
  20.5 8.2 %copy-start.4 = (bf16[8,320]{1,0:T(8,128)(2,1)S(1)}, bf16[8,320]{1,0:T(8,128)(2,1)}, u32[]{:S(2)}) copy-start(bf16[8,320]{1,0:T(8,128)(2,1)} %param.16) | copy-start | bytes 15364
  20.5 300.0 %all-to-all-start = ((bf16[16,8,1,128,256]{4,3,1,2,0:T(8,128)(2,1)}), bf16[16,8,1,128,256]{4,3,1,2,0:T(8,128)(2,1)}, u32[]{:S(2)}, u32[]{:S(2)}) async-start(bf16[16,8,1,128,256]{4,3,1,2,0:T(8,128)(2,1)} %bitcast.81), calls=%async_computation | async-start | bytes 16777216 | tf_op jit(solution)/shard_map/all_to_all | solution.py:107
  27.8 96.8 %all-reduce.5.cloned.1.call-start = ((), (), s32[]{:S(2)}) async-start(), calls=%async_computation.1 | async-start | bytes 163840 | tf_op jit(solution)/shard_map/psum | solution.py:137
  45.4 5.1 %copy-start.3 = (bf16[2560,128]{1,0:T(8,128)(2,1)S(1)}, bf16[2560,128]{1,0:T(8,128)(2,1)}, u32[]{:S(2)}) copy-start(bf16[2560,128]{1,0:T(8,128)(2,1)} %param.20) | copy-start | bytes 1966084
  60.5 5.7 %copy-start.7 = (s32[128]{0:T(128)S(1)}, s32[128]{0:T(128)}, u32[]{:S(2)}) copy-start(s32[128]{0:T(128)} %param.31) | copy-start | bytes 1540
  60.6 5.9 %copy-start.6 = (bf16[320]{0:T(512)(128)(2,1)S(1)}, bf16[320]{0:T(512)(128)(2,1)}, u32[]{:S(2)}) copy-start(bf16[320]{0:T(512)(128)(2,1)} %param.24) | copy-start | bytes 1924
  60.6 6.7 %copy-start.11 = (u32[128]{0:T(128)S(1)}, u32[128]{0:T(128)}, u32[]{:S(2)}) copy-start(u32[128]{0:T(128)} %constant.91) | copy-start | bytes 1540
  60.6 106.4 %copy-start.8 = (bf16[320,608]{1,0:T(8,128)(2,1)S(1)}, bf16[320,608]{1,0:T(8,128)(2,1)}, u32[]{:S(2)}) copy-start(bf16[320,608]{1,0:T(8,128)(2,1)} %param.26) | copy-start | bytes 1167364
  66.2 166.5 %all-reduce.7.cloned.1.call-start = ((), (), s32[]{:S(2)}) async-start(), calls=%async_computation.2 | async-start | bytes 1245184 | tf_op jit(solution)/shard_map/psum | solution.py:156
  169.6 149.6 %all-reduce.9.cloned.1.call-start = ((), (), s32[]{:S(2)}) async-start(), calls=%async_computation.3 | async-start | bytes 393216
Sparse Core Ops, SparseCore 0:
  66.4 58.2 all-reduce.4
  169.7 62.9 all-reduce.6
  236.5 82.5 all-reduce.8
where the time goes:
time: 342 us; the launch traced here: 341 us
  waiting for transfers between devices  203 us (59%)
  blocking collectives  55.1 us (16%)
  local copies, waits for them, and re-layouts  26.1 us (8%)
  other arithmetic  20.4 us (6%)
  between operations  14.7 us (4%)
  matrix products  14.3 us (4%)
  starting transfers between devices  7.46 us (2%)
    unnamed x4, waiting for transfers between devices  84.2 us
    psum x1, waiting for transfers between devices, per_device(): summed = lax.psum(partial_both, 'kvh')  62.3 us
    psum x1, waiting for transfers between devices, per_device(): attn_out = lax.psum(partial_out, 'kvh')  56.2 us
    all_gather x1, blocking collectives, per_device(): lax.all_gather(jnp.concatenate([normed_two, fresh_flat], axis=1), 'req',...  41 us
    select_n x2, other arithmetic, mask_blocks(): jnp.where(kept, blocks, jnp.where(placed, fresh[:, None, :, None, :], jnp...  15.3 us
    all_gather x1, blocking collectives, per_device(): full_states = lax.all_gather(states, 'kvh', axis=1, tiled=True)  14 us
    gather x3, local copies, waits for them, and re-layouts, per_device(): parcels = kv_pool[page_table[picked]]  9.99 us
    all_to_all x1, starting transfers between devices, per_device(): lax.all_to_all(parcels, 'req', split_axis=0, concat_axis=0, tiled=True)  7.34 us
  transfers between devices with their start and end apart: 4, of which 3 were waited for; matrix products, arithmetic and copies ran while one was open for 10% of the time, Pallas kernels for 0%

commit v1 on v0

--- a/solution.py
+++ b/solution.py
@@ -107,7 +107,23 @@
     received = lax.all_to_all(parcels, "req", split_axis=0, concat_axis=0, tiled=True)
     arriving = lax.dynamic_slice_in_dim(new_order, my_index * row_count, row_count)
     source_owner = arriving // row_count
-    full_states = lax.all_gather(states, "kvh", axis=1, tiled=True)
+    size, index, width = (lax.axis_size("kvh"), lax.axis_index("kvh"), states.shape[1])
+    upward = [(i, (i + 1) % size) for i in range(size)]
+    behind = [(i, (i - 1) % size) for i in range(size)]
+    full_states = jnp.zeros((*states.shape[:1], size * width, *states.shape[1 + 1 :]), states.dtype)
+    full_states = lax.dynamic_update_slice_in_dim(full_states, states, index * width, axis=1)
+    from_left = from_right = states
+    halfway = size // 2
+    for step in range(1, halfway + 1):
+        from_left = lax.ppermute(from_left, "kvh", upward)
+        full_states = lax.dynamic_update_slice_in_dim(
+            full_states, from_left, (index - step) % size * width, axis=1
+        )
+        if step < size - halfway:
+            from_right = lax.ppermute(from_right, "kvh", behind)
+            full_states = lax.dynamic_update_slice_in_dim(
+                full_states, from_right, (index + step) % size * width, axis=1
+            )
     normed = rms_norm(full_states.astype(jnp.float32), attn_gain.astype(jnp.float32)).astype(
         jnp.bfloat16
     )

time: 342 us -> 342 us (level)
  blocking collectives: 55.1 us -> 37.6 us
  starting transfers between devices: 7.46 us -> 16.9 us
  waiting for transfers between devices: 203 us -> 208 us
    all_gather x1 -> x0, blocking collectives: 14 us -> none  [per_device(): full_states = lax.all_gather(states, 'kvh', axis=1, tiled=True)]
    ppermute x0 -> x7, starting transfers between devices: none -> 9.47 us  [the longest x3 9.46 us: per_device(): from_right = lax.ppermute(from_right, 'kvh', behind)]
    ppermute x0 -> x7, waiting for transfers between devices: none -> 5.39 us  [the longest x4 5.38 us: per_device(): from_left = lax.ppermute(from_left, 'kvh', upward)]
  transfers between devices with their start and end apart: 4 -> 11, of which waited for: 3 -> 6; matrix products, arithmetic and copies ran while one was open for 10% -> 11% of each run, Pallas kernels for 0% -> 0%
where the time goes in v1:
time: 342 us; the launch traced here: 341 us
  waiting for transfers between devices  208 us (61%)
  blocking collectives  37.6 us (11%)
  local copies, waits for them, and re-layouts  28.4 us (8%)
  other arithmetic  20.4 us (6%)
  starting transfers between devices  16.9 us (5%)
  between operations  14.8 us (4%)
  matrix products  14.5 us (4%)
    unnamed x4, waiting for transfers between devices  84.2 us
    psum x1, waiting for transfers between devices, per_device(): summed = lax.psum(partial_both, 'kvh')  62.3 us
    psum x1, waiting for transfers between devices, per_device(): attn_out = lax.psum(partial_out, 'kvh')  56.4 us
    all_gather x1, blocking collectives, per_device(): lax.all_gather(jnp.concatenate([normed_two, fresh_flat], axis=1), 'req',...  37.6 us
    select_n x2, other arithmetic, mask_blocks(): jnp.where(kept, blocks, jnp.where(placed, fresh[:, None, :, None, :], jnp...  15.3 us
    gather x3, local copies, waits for them, and re-layouts, per_device(): parcels = kv_pool[page_table[picked]]  9.99 us
    ppermute x3, starting transfers between devices, per_device(): from_right = lax.ppermute(from_right, 'kvh', behind)  9.46 us
    all_to_all x1, starting transfers between devices, per_device(): lax.all_to_all(parcels, 'req', split_axis=0, concat_axis=0, tiled=True)  7.34 us
  transfers between devices with their start and end apart: 11, of which 6 were waited for; matrix products, arithmetic and copies ran while one was open for 11% of the time, Pallas kernels for 0%

profile of v1, /device:TPU:0, one launch (start us, length us, event | category | flops | bytes accessed | tf_op | source)
XLA Modules:
  0.0 340.9 jit_solution(18242022822348772223)
XLA Ops:
  10.3 1.2 gather_fusion.4
  11.8 8.7 %gather_fusion.5 = bf16[128,128,256]{2,1,0:T(8,128)(2,1)} fusion(bf16[64,128,256]{2,1,0:T(8,128)(2,1)} %bitcast.56, s32[1024]{0:T(1024)S(1)} %pad_clamp_fusion.1), kind=kCustom, calls=%fused_computation.5 | custom fusion | bytes 16777728 | tf_op jit(solution)/shard_map/gather | solution.py:106
  20.5 7.3 %all-to-all-start = ((bf16[16,8,1,128,256]{4,3,1,2,0:T(8,128)(2,1)}), bf16[16,8,1,128,256]{4,3,1,2,0:T(8,128)(2,1)}, u32[]{:S(2)}, u32[]{:S(2)}) async-start(bf16[16,8,1,128,256]{4,3,1,2,0:T(8,128)(2,1)} %bitcast.58), calls=%async_computation | async-start | bytes 16777216 | tf_op jit(solution)/shard_map/all_to_all | solution.py:107
  27.9 3.2 collective-permute-start.1
  32.2 3.2 collective-permute-done
  35.4 3.0 collective-permute-start.3
  38.4 1.3 collective-permute-done.2
  39.8 3.3 collective-permute-start.5
  44.0 5.1 %gather_fusion.1 = bf16[64,128,256]{2,1,0:T(8,128)(2,1)} fusion(bf16[64,128,256]{2,1,0:T(8,128)(2,1)} %bitcast.57, s32[1024]{0:T(1024)S(1)} %pad_clamp_fusion.4), kind=kCustom, calls=%fused_computation.1 | custom fusion | bytes 8388864 | tf_op jit(solution)/shard_map/gather | solution.py:147
  51.7 2.3 multiply_reduce_fusion.1
  54.4 1.5 multiply_reduce_fusion.2
  56.3 7.6 %select_select_fusion.1 = bf16[8,1,1024,256]{3,2,0,1:T(8,128)(2,1)} fusion(bf16[8,1,1024,256]{3,2,0,1:T(8,128)(2,1)} %bitcast.60, pred[8,1024]{1,0:T(8,128)(4,1)S(1)} %get-tuple-element.13, pred[8,1024]{1,0:T(8,128)(4,1)S(1)} %get-tuple-element.12, bf16[8,256]{1,0:T(8,128)(2,1)S(1)} %maximum_bitcast_fusion), kind=kLoop, calls=%fused_computation.11 | loop fusion | flops 4194304 | bytes 8409088 | tf_op jit(solution)/shard_map/jit(_where)/select_n | solution.py:45
  63.9 2.5 fusion.52
  66.4 2.0 fusion.8
  68.5 1.1 fusion.26
  71.7 56.4 %all-reduce.5.cloned.1.call-done = f32[8,2560]{1,0:T(8,128)} async-done(((f32[8,2560]{1,0:T(8,128)}), f32[8,2560]{1,0:T(8,128)}) %all-reduce.5.cloned.1.call-update) | async-done | bytes 81936 | tf_op jit(solution)/shard_map/psum | solution.py:153
  129.3 37.6 %all_gather.3 = bf16[128,576]{1,0:T(8,128)(2,1)S(1)} all-gather(bf16[8,576]{1,0:T(8,128)(2,1)S(1)} %pad_maximum_fusion), channel_id=1, replica_groups=mesh['req'=16,'kvh'=8] {'req'}, dimensions={0}, use_global_device_ids=true | all-gather | bytes 156672 | tf_op jit(solution)/shard_map/all_gather | solution.py:164
  166.9 2.7 fusion.10
  170.4 62.3 %all-reduce.7.cloned.1.call-done = f32[128,1216]{0,1:T(8,128)} async-done(((f32[128,1216]{0,1:T(8,128)}), f32[128,1216]{0,1:T(8,128)}) %all-reduce.7.cloned.1.call-update) | async-done | bytes 622608 | tf_op jit(solution)/shard_map/psum | solution.py:172
  232.8 2.2 fusion.15
  235.0 84.2 %all-reduce.9.cloned.1.call-done = f32[128,320]{1,0:T(8,128)} async-done(((f32[128,320]{1,0:T(8,128)}), f32[128,320]{1,0:T(8,128)}) %all-reduce.9.cloned.1.call-update) | async-done | bytes 163856
  319.2 1.4 fusion.25
  320.5 6.2 %gather_fusion.6 = bf16[8,8,128,256]{3,2,1,0:T(8,128)(2,1)} fusion(bf16[16,8,128,256]{3,2,1,0:T(8,128)(2,1)} %bitcast.13, s32[1024]{0:T(1024)S(1)} %pad_clamp_fusion), kind=kCustom, calls=%fused_computation.6 | custom fusion | bytes 8388640 | tf_op jit(solution)/shard_map/gather | solution.py:181
  326.8 7.6 %select_select_fusion = bf16[64,1,128,256]{3,2,1,0:T(8,128)(2,1)} fusion(bf16[64,1,128,256]{3,2,1,0:T(8,128)(2,1)} %bitcast.59, pred[64,128]{1,0:T(8,128)(4,1)S(1)} %get-tuple-element.11, pred[64,128]{1,0:T(8,128)(4,1)S(1)} %get-tuple-element.10, bf16[64,256]{1,0:T(8,128)(2,1)S(1)} %broadcast_bitcast_fusion), kind=kLoop, calls=%fused_computation.10 | loop fusion | flops 4194304 | bytes 8437760 | tf_op jit(solution)/shard_map/jit(_where)/select_n | solution.py:45
  (104 shorter events, 12.2 us)
Async XLA Ops:
  7.2 61.3 %copy-start = (bf16[512,2560]{1,0:T(8,128)(2,1)S(1)}, bf16[512,2560]{1,0:T(8,128)(2,1)}, u32[]{:S(2)}) copy-start(bf16[512,2560]{1,0:T(8,128)(2,1)} %param.23) | copy-start | bytes 7864324
  20.5 7.4 %copy-start.5 = (bf16[8,320]{1,0:T(8,128)(2,1)S(1)}, bf16[8,320]{1,0:T(8,128)(2,1)}, u32[]{:S(2)}) copy-start(bf16[8,320]{1,0:T(8,128)(2,1)} %param.16) | copy-start | bytes 15364
  20.5 10.7 %copy-start.1 = (s32[128]{0:T(128)S(1)}, s32[128]{0:T(128)}, u32[]{:S(2)}) copy-start(s32[128]{0:T(128)} %param.29) | copy-start | bytes 1540
  20.5 11.6 %copy-start.2 = (s32[8,8]{1,0:T(8,128)S(1)}, s32[8,8]{1,0:T(8,128)}, u32[]{:S(2)}) copy-start(s32[8,8]{1,0:T(8,128)} %param.30) | copy-start | bytes 772
  20.5 19.2 %copy-start.7 = (s32[128]{0:T(128)S(1)}, s32[128]{0:T(128)}, u32[]{:S(2)}) copy-start(s32[128]{0:T(128)} %param.31) | copy-start | bytes 1540
  20.5 23.5 %copy-start.9 = (bf16[128]{0:T(256)(128)(2,1)S(1)}, bf16[128]{0:T(256)(128)(2,1)}, u32[]{:S(2)}) copy-start(bf16[128]{0:T(256)(128)(2,1)} %param.21) | copy-start | bytes 772
  20.5 23.5 %copy-start.10 = (bf16[128]{0:T(256)(128)(2,1)S(1)}, bf16[128]{0:T(256)(128)(2,1)}, u32[]{:S(2)}) copy-start(bf16[128]{0:T(256)(128)(2,1)} %param.22) | copy-start | bytes 772
  20.5 23.5 %copy-start.4 = (bf16[2560]{0:T(1024)(128)(2,1)S(1)}, bf16[2560]{0:T(1024)(128)(2,1)}, u32[]{:S(2)}) copy-start(bf16[2560]{0:T(1024)(128)(2,1)} %param.17) | copy-start | bytes 15364
  20.5 300.0 %all-to-all-start = ((bf16[16,8,1,128,256]{4,3,1,2,0:T(8,128)(2,1)}), bf16[16,8,1,128,256]{4,3,1,2,0:T(8,128)(2,1)}, u32[]{:S(2)}, u32[]{:S(2)}) async-start(bf16[16,8,1,128,256]{4,3,1,2,0:T(8,128)(2,1)} %bitcast.58), calls=%async_computation | async-start | bytes 16777216 | tf_op jit(solution)/shard_map/all_to_all | solution.py:107
  27.9 100.2 %all-reduce.5.cloned.1.call-start = ((), (), s32[]{:S(2)}) async-start(), calls=%async_computation.1 | async-start | bytes 163840 | tf_op jit(solution)/shard_map/psum | solution.py:153
  27.9 7.5 %collective-permute-start.1 = (bf16[8,320]{1,0:T(8,128)(2,1)S(1)}, bf16[8,320]{1,0:T(8,128)(2,1)S(1)}, u32[]{:S(2)}, u32[]{:S(2)}) collective-permute-start(bf16[8,320]{1,0:T(8,128)(2,1)S(1)} %copy-done.5), channel_id=1, source_target_pairs={{0,7},{1,0},{2,1},{3,2},{4,3},{5,4},{6,5},{7,6},{8,15},{9,8},{10,9... | collective-permute-start | bytes 15368 | tf_op jit(solution)/shard_map/ppermute | solution.py:123
  31.1 4.3 %collective-permute-start = (bf16[8,320]{1,0:T(8,128)(2,1)S(1)}, bf16[8,320]{1,0:T(8,128)(2,1)S(1)}, u32[]{:S(2)}, u32[]{:S(2)}) collective-permute-start(bf16[8,320]{1,0:T(8,128)(2,1)S(1)} %copy-done.5), channel_id=1, source_target_pairs={{0,1},{1,2},{2,3},{3,4},{4,5},{5,6},{6,7},{7,0},{8,9},{9,10},{10,1... | collective-permute-start | bytes 15368 | tf_op jit(solution)/shard_map/ppermute | solution.py:118
  35.4 4.3 %collective-permute-start.2 = (bf16[8,320]{1,0:T(8,128)(2,1)S(1)}, bf16[8,320]{1,0:T(8,128)(2,1)S(1)}, u32[]{:S(2)}, u32[]{:S(2)}) collective-permute-start(bf16[8,320]{1,0:T(8,128)(2,1)S(1)} %collective-permute-done), channel_id=1, source_target_pairs={{0,1},{1,2},{2,3},{3,4},{4,5},{5,6},{6,7},{7,0},{8,9},{9,10},{10,1... | collective-permute-start | bytes 15368 | tf_op jit(solution)/shard_map/ppermute | solution.py:118
  35.4 4.3 %collective-permute-start.3 = (bf16[8,320]{1,0:T(8,128)(2,1)S(1)}, bf16[8,320]{1,0:T(8,128)(2,1)S(1)}, u32[]{:S(2)}, u32[]{:S(2)}) collective-permute-start(bf16[8,320]{1,0:T(8,128)(2,1)S(1)} %collective-permute-done.1), channel_id=1, source_target_pairs={{0,7},{1,0},{2,1},{3,2},{4,3},{5,4},{6,5},{7,6},{8,15},{9,8},{10,9... | collective-permute-start | bytes 15368 | tf_op jit(solution)/shard_map/ppermute | solution.py:123
  39.7 4.3 %collective-permute-start.4 = (bf16[8,320]{1,0:T(8,128)(2,1)S(1)}, bf16[8,320]{1,0:T(8,128)(2,1)S(1)}, u32[]{:S(2)}, u32[]{:S(2)}) collective-permute-start(bf16[8,320]{1,0:T(8,128)(2,1)S(1)} %collective-permute-done.2), channel_id=1, source_target_pairs={{0,1},{1,2},{2,3},{3,4},{4,5},{5,6},{6,7},{7,0},{8,9},{9,10},{10,1... | collective-permute-start | bytes 15368 | tf_op jit(solution)/shard_map/ppermute | solution.py:118
  39.8 11.1 %collective-permute-start.5 = (bf16[8,320]{1,0:T(8,128)(2,1)S(1)}, bf16[8,320]{1,0:T(8,128)(2,1)S(1)}, u32[]{:S(2)}, u32[]{:S(2)}) collective-permute-start(bf16[8,320]{1,0:T(8,128)(2,1)S(1)} %collective-permute-done.3), channel_id=1, source_target_pairs={{0,7},{1,0},{2,1},{3,2},{4,3},{5,4},{6,5},{7,6},{8,15},{9,8},{10,9... | collective-permute-start | bytes 15368 | tf_op jit(solution)/shard_map/ppermute | solution.py:123
  43.9 7.3 %collective-permute-start.6 = (bf16[8,320]{1,0:T(8,128)(2,1)S(1)}, bf16[8,320]{1,0:T(8,128)(2,1)S(1)}, u32[]{:S(2)}, u32[]{:S(2)}) collective-permute-start(bf16[8,320]{1,0:T(8,128)(2,1)S(1)} %collective-permute-done.4), channel_id=1, source_target_pairs={{0,1},{1,2},{2,3},{3,4},{4,5},{5,6},{6,7},{7,0},{8,9},{9,10},{10,1... | collective-permute-start | bytes 15368 | tf_op jit(solution)/shard_map/ppermute | solution.py:118
  44.0 10.1 %copy-start.3 = (bf16[2560,128]{1,0:T(8,128)(2,1)S(1)}, bf16[2560,128]{1,0:T(8,128)(2,1)}, u32[]{:S(2)}) copy-start(bf16[2560,128]{1,0:T(8,128)(2,1)} %param.20) | copy-start | bytes 1966084
  63.9 5.7 %copy-start.6 = (bf16[320]{0:T(512)(128)(2,1)S(1)}, bf16[320]{0:T(512)(128)(2,1)}, u32[]{:S(2)}) copy-start(bf16[320]{0:T(512)(128)(2,1)} %param.24) | copy-start | bytes 1924
  63.9 6.6 %copy-start.11 = (u32[128]{0:T(128)S(1)}, u32[128]{0:T(128)}, u32[]{:S(2)}) copy-start(u32[128]{0:T(128)} %constant.137) | copy-start | bytes 1540
  63.9 103.0 %copy-start.8 = (bf16[320,608]{1,0:T(8,128)(2,1)S(1)}, bf16[320,608]{1,0:T(8,128)(2,1)}, u32[]{:S(2)}) copy-start(bf16[320,608]{1,0:T(8,128)(2,1)} %param.26) | copy-start | bytes 1167364
  69.6 163.2 %all-reduce.7.cloned.1.call-start = ((), (), s32[]{:S(2)}) async-start(), calls=%async_computation.2 | async-start | bytes 1245184 | tf_op jit(solution)/shard_map/psum | solution.py:172
  169.6 149.6 %all-reduce.9.cloned.1.call-start = ((), (), s32[]{:S(2)}) async-start(), calls=%async_computation.3 | async-start | bytes 393216
Sparse Core Ops, SparseCore 0:
  69.7 58.3 all-reduce.4
  169.7 62.9 all-reduce.6
  236.6 82.5 all-reduce.8
